TPU v7x, 512 devices: a whole 4x4x16 slice. The times are simulated.
512 devices in a mesh: tok: 16 (over z), head: 32 (over y, x, core).
Axes of the slice: x: 4, y: 4, z: 16, core: 2. Of those that a mesh axis runs over, the one named last changes fastest.
Arguments:
- tokens: bfloat16 [3072, 4096], P(('tok', 'head')), may hold values from -6 to 6
- ln1_gain: float32 [4096], replicated, may hold values from 0.25 to 1.75
- ln1_bias: float32 [4096], replicated, may hold values from -1.75 to 1.75
- ln2_gain: float32 [4096], replicated, may hold values from 0.25 to 1.75
- ln2_bias: float32 [4096], replicated, may hold values from -1.75 to 1.75
- w_qkv: bfloat16 [4096, 12288], P('tok', 'head'), may hold values from -0.09375 to 0.09375
- b_qkv: float32 [12288], P('head'), may hold values from -3 to 3
- w_dense: bfloat16 [4096, 4096], P('head', 'tok'), may hold values from -0.09375 to 0.09375
- b_dense: float32 [4096], replicated, may hold values from -1.75 to 1.75
- w_up: bfloat16 [4096, 16384], P('tok', 'head'), may hold values from -0.09375 to 0.09375
- b_up: float32 [16384], P('head'), may hold values from -3 to 3
- w_down: bfloat16 [16384, 4096], P('head', 'tok'), may hold values from -0.046875 to 0.046875
- b_down: float32 [4096], replicated, may hold values from -1.75 to 1.75
- k_cache: bfloat16 [98304, 4096], P('tok', 'head'), may hold values from -610 to 610
- v_cache: bfloat16 [98304, 4096], P('tok', 'head'), may hold values from -6 to 6
- cache_lengths: int32 [16, 33], P('tok'), may hold values from 1 to 4096, 6144 in all within a row
Outputs:
- mixed: bfloat16 [3072, 4096], P(('tok', 'head'))
Inputs may be any that keep to these rules, and one draw needn't show every extreme that they name: `cache_lengths`: row g lists the cache lengths of group g's 33 requests in the order in which their caches lie in the group's 6144 cache rows; every row sums to 6144. Request 0 of a group is the one whose 160 new tokens are prefilled, the others decode one token each.
All inputs are finite; a program needn't handle non-finite values.
Results may differ from a plain program's by a relative error of at most 0.02.
Values may be sent and summed in bfloat16 or wider, within the bound.
No kernel may reach another device: no remote copies, remote signals or barrier semaphores. Data moves between devices by JAX's collectives and lax.ppermute only.
A program may use at most 64 MiB of HBM per device.

v0:
```python
import jax
import jax.numpy as jnp
from jax import lax
from jax.sharding import PartitionSpec as P

HD = 128
ROT = 32
WINDOW = 2048
SINKS = 4


epsilon = 1e-05


def layer_norm(values, gain, shift):
    values = values.astype(jnp.float32)
    center = jnp.mean(values, axis=-1, keepdims=True)
    spread = jnp.mean(jnp.square(values - center), axis=-1, keepdims=True)
    return (values - center) * lax.rsqrt(spread + epsilon) * gain + shift


def rotate(values, positions):
    half = ROT // 2
    inverse = jnp.power(jnp.float32(10000.0), -jnp.arange(half, dtype=jnp.float32) * (2.0 / ROT))
    angles = (
        positions.astype(jnp.float32).reshape(positions.shape + (1,) * (values.ndim - 1)) * inverse
    )
    cosine = jnp.cos(angles)
    sine = jnp.sin(angles)
    first = values[..., :half]
    second = values[..., half:ROT]
    rest = values[..., ROT:]
    return jnp.concatenate(
        [first * cosine - second * sine, second * cosine + first * sine, rest], axis=-1
    )


def token_layout(lengths_row, group_rows):
    requests_count = lengths_row.shape[0]
    count_pre = group_rows - (requests_count - 1)
    index = jnp.arange(group_rows, dtype=jnp.int32)
    owner = jnp.maximum(index - (count_pre - 1), 0)
    table = owner[:, None] == jnp.arange(requests_count, dtype=jnp.int32)[None, :]
    start = jnp.sum(jnp.where(table, lengths_row[None, :], 0), axis=1)
    place = start + jnp.where(owner == 0, index, 0)
    return (owner, place)


def slot_layout(lengths_row, slots):
    starts = jnp.cumsum(lengths_row) - lengths_row
    index = jnp.arange(slots, dtype=jnp.int32)
    inside = index[:, None] >= starts[None, :]
    owner = jnp.sum(inside.astype(jnp.int32), axis=1) - 1
    begin = jnp.max(jnp.where(inside, starts[None, :], 0), axis=1)
    return (owner, index - begin)


def visible(query_owner, query_place, key_owner, key_place):
    same = query_owner[:, None] == key_owner[None, :]
    before = key_place[None, :] <= query_place[:, None]
    near = (key_place[None, :] < SINKS) | (query_place[:, None] - key_place[None, :] < WINDOW)
    return same & before & near


def body(
    tokens,
    ln1_gain,
    ln1_bias,
    ln2_gain,
    ln2_bias,
    w_qkv,
    b_qkv,
    w_dense,
    b_dense,
    w_up,
    b_up,
    w_down,
    b_down,
    k_cache,
    v_cache,
    cache_lengths,
):
    scale = HD ** (-0.5)
    whole = lax.all_gather(tokens, "head", axis=0, tiled=True)
    normed_one = layer_norm(whole, ln1_gain, ln1_bias).astype(jnp.bfloat16)
    normed_two = layer_norm(whole, ln2_gain, ln2_bias).astype(jnp.bfloat16)
    rows_total = whole.shape[0]
    projected = jnp.dot(
        normed_one,
        lax.all_gather(w_qkv, "tok", axis=0, tiled=True),
        preferred_element_type=jnp.float32,
    )
    upward = jnp.dot(
        normed_two,
        lax.all_gather(w_up, "tok", axis=0, tiled=True),
        preferred_element_type=jnp.float32,
    )
    projected = projected + b_qkv
    lengths_row = cache_lengths[0]
    query_owner, query_place = token_layout(lengths_row, rows_total)
    queries = rotate(projected[:, :HD], query_place).astype(jnp.bfloat16)
    new_keys = rotate(projected[:, HD : 2 * HD], query_place).astype(jnp.bfloat16)
    new_values = projected[:, 2 * HD :].astype(jnp.bfloat16)
    hidden = jax.nn.gelu(upward + b_up, approximate=False).astype(jnp.bfloat16)
    slots = k_cache.shape[0]
    slot_owner, slot_place = slot_layout(lengths_row, slots)
    block = 512
    while slots % block:
        block = block // 2
    number = slots // block
    indices = jnp.arange(number, dtype=jnp.int32)
    key_blocks = k_cache.reshape(number, block, HD)
    value_blocks = v_cache.reshape(number, block, HD)
    owner_blocks = slot_owner.reshape(number, block)
    place_blocks = slot_place.reshape(number, block)
    new_scores = jnp.dot(queries, new_keys.T, preferred_element_type=jnp.float32) * scale
    new_scores = jnp.where(
        visible(query_owner, query_place, query_owner, query_place), new_scores, -jnp.inf
    )

    def first_pass(top, items):
        index, keys, block_owner, block_place = items
        raw = jnp.dot(queries, keys.T, preferred_element_type=jnp.float32) * scale
        scores = jnp.where(
            visible(query_owner, query_place, block_owner, block_place), raw, -jnp.inf
        )
        return (jnp.maximum(top, jnp.max(scores, axis=1)), scores)

    top, stored = lax.scan(
        first_pass, jnp.max(new_scores, axis=1), (indices, key_blocks, owner_blocks, place_blocks)
    )
    new_weights = jnp.exp(new_scores - top[:, None])
    start_state = (
        jnp.sum(new_weights, axis=1),
        jnp.dot(new_weights.astype(jnp.bfloat16), new_values, preferred_element_type=jnp.float32),
    )

    def second_pass(state, items):
        index, scores, values = items
        weights = jnp.exp(scores - top[:, None])
        state = (
            state[0] + jnp.sum(weights, axis=1),
            state[1]
            + jnp.dot(weights.astype(jnp.bfloat16), values, preferred_element_type=jnp.float32),
        )
        return (state, None)

    final, unused = lax.scan(second_pass, start_state, (indices, stored, value_blocks))
    attention = (final[1] / final[0][:, None]).astype(jnp.bfloat16)
    dense_full, down_full = (
        lax.all_gather(w_dense, "tok", axis=1, tiled=True),
        lax.all_gather(w_down, "tok", axis=1, tiled=True),
    )
    partial_value = lax.psum_scatter(
        (
            jnp.dot(attention, dense_full, preferred_element_type=jnp.float32)
            + jnp.dot(hidden, down_full, preferred_element_type=jnp.float32)
        ).astype(jnp.bfloat16),
        "head",
        scatter_dimension=0,
        tiled=True,
    ).astype(jnp.float32)
    mixed = tokens.astype(jnp.float32) + partial_value + b_dense + b_down
    return mixed.astype(jnp.bfloat16)


def solution(mesh):
    placed = (
        P(("tok", "head"), None),
        P(),
        P(),
        P(),
        P(),
        P("tok", "head"),
        P("head"),
        P("head", "tok"),
        P(),
        P("tok", "head"),
        P("head"),
        P("head", "tok"),
        P(),
        P("tok", "head"),
        P("tok", "head"),
        P("tok", None),
    )
    return jax.shard_map(
        body, mesh=mesh, in_specs=placed, out_specs=P(("tok", "head"), None), check_vma=False
    )
```

profile of v0, /device:TPU:1, one launch (start us, length us, event | category | flops | bytes accessed | tf_op | source)
XLA Modules:
  0.0 514.6 jit_solution(13324093084957807305)
XLA Ops:
  14.9 60.5 %all-gather.15.cloned.1.call-done = bf16[32,6,4096]{2,1,0:T(8,128)(2,1)} async-done(((bf16[1,6,4096]{2,1,0:T(8,128)(2,1)}), bf16[32,6,4096]{2,1,0:T(8,128)(2,1)}) %all-gather.15.cloned.1.call-update) | async-done | bytes 1572880 | tf_op jit(solution)/shard_map/all_gather | solution.py:84
  75.4 2.1 convert_reduce_fusion
  77.6 2.5 reshape.102
  80.6 63.4 %all-gather.7.cloned.1.call-done = bf16[4096,384]{1,0:T(8,128)(2,1)} async-done(((bf16[256,384]{1,0:T(8,128)(2,1)}), bf16[4096,384]{1,0:T(8,128)(2,1)}) %all-gather.7.cloned.1.call-update) | async-done | bytes 3145744 | tf_op jit(solution)/shard_map/all_gather | solution.py:90
  144.0 3.4 fusion.139
  150.7 34.4 %while.26 = (s32[]{:T(128)}, f32[192]{0:T(256)S(1)}, f32[12,192,512]{2,1,0:T(8,128)}, s32[12,512]{1,0:T(8,128)}, s32[12,512]{1,0:T(8,128)S(1)}, /*index=5*/s32[1...) while((s32[]{:T(128)}, f32[192]{0:T(256)S(1)}, ...), condition=%wide.region_9.10_spmd.clone, body=%wide.region_7.9_spmd.clone.sunk | while | flops 26149760 | bytes 1379941 | solution.py:129
  151.5 1.3 fusion.155
  154.3 1.3 fusion.155
  157.2 1.3 fusion.155
  160.1 1.3 fusion.155
  162.9 1.3 fusion.155
  165.8 1.3 fusion.155
  168.7 1.3 fusion.155
  171.5 1.3 fusion.155
  174.4 1.3 fusion.155
  177.2 1.3 fusion.155
  180.1 1.3 fusion.155
  183.0 1.3 fusion.155
  186.2 30.5 %while.25 = (s32[]{:T(128)}, f32[192]{0:T(256)S(1)}, f32[192,128]{1,0:T(8,128)S(1)}, f32[12,192,512]{2,1,0:T(8,128)}, f32[192]{0:T(256)S(1)}, /*index=5*/bf16[12,512,128]{2,1,0:T(8,128)(2,1)}, s32[]{:T(128)}) while((s32[]{:T(128)}, f32[192]{0:T(256)S(1)}, f32[192,128]{1,0:T(8,128)S(1)}, f32[12,192,512]{2,1,0:T(8,128)}, f32[192]{0:T(256)S(1)}, ...), condition=%wide.region_13.14_spmd, body=%wide.region_11.13_spmd.sunk | while | flops 25583616 | bytes 1119825 | solution.py:148
  188.7 1.3 convolution_add_fusion.3
  206.5 1.3 convolution_add_fusion.3
  216.8 3.5 fusion.86
  220.3 71.5 %all-gather.11.cloned.1.call-done = bf16[4096,512]{1,0:T(8,128)(2,1)} async-done(((bf16[256,512]{1,0:T(8,128)(2,1)}), bf16[4096,512]{1,0:T(8,128)(2,1)}) %all-gather.11.cloned.1.call-update) | async-done | bytes 4194320 | tf_op jit(solution)/shard_map/all_gather | solution.py:95
  291.8 92.5 %all-gather.13.cloned.1.call-done = bf16[512,4096]{1,0:T(8,128)(2,1)} async-done(((bf16[512,256]{1,0:T(8,128)(2,1)}), bf16[512,4096]{1,0:T(8,128)(2,1)}) %all-gather.13.cloned.1.call-update) | async-done | bytes 4194320 | tf_op jit(solution)/shard_map/all_gather | solution.py:152
  384.3 8.3 %fusion.18 = bf16[192,4096]{1,0:T(8,128)(2,1)} fusion(f32[192,4096]{1,0:T(8,128)} %fusion.86, bf16[512,4096]{1,0:T(8,128)(2,1)} %all-gather.13.cloned.1.call-done, bf16[4096,512]{1,0:T(8,128)(2,1)} %all-gather.11.cloned.1.call-done, f32[192,4096]{1,0:T(8,128)S(1)} %reshape.102, f32[4096]{0:T(1024)S(1)} %copy-done.9, f32[4096]{0:T(1024)S(1)} %copy-done.10, ...), kind=kOutput, calls=%fused_computation.26 | convolution fusion | flops 1622605824 | bytes 16289280 | tf_op jit(solution)/shard_map/dot_general | solution.py:157
  392.6 84.4 %fusion.2 = bf16[8,4096]{1,0:T(8,128)(2,1)S(1)} fusion(bf16[192,4096]{1,0:T(8,128)(2,1)} %fusion.18), kind=kCustom, calls=%all-reduce-scatter | all-reduce-scatter fusion | flops 1048577 | bytes 1640448
  477.1 3.5 collective-permute-start
  484.5 2.3 collective-permute-start.3
  486.8 5.5 %collective-permute-start.4 = (bf16[8,4096]{1,0:T(8,128)(2,1)S(1)}, bf16[8,4096]{1,0:T(8,128)(2,1)S(1)}, u32[]{:S(2)}, u32[]{:S(2)}) collective-permute-start(bf16[8,4096]{1,0:T(8,128)(2,1)S(1)} %fusion.2), channel_id=1, source_target_pairs={{0,5},{1,6},{2,7},{3,8},{4,9},{5,10},{6,11},{7,12},{8,13},{9,14},{... | collective-permute-start | bytes 196616
  492.3 5.1 collective-permute-start.5
  497.4 6.4 %collective-permute-start.6 = (bf16[8,4096]{1,0:T(8,128)(2,1)S(1)}, bf16[8,4096]{1,0:T(8,128)(2,1)S(1)}, u32[]{:S(2)}, u32[]{:S(2)}) collective-permute-start(bf16[8,4096]{1,0:T(8,128)(2,1)S(1)} %fusion.2), channel_id=1, source_target_pairs={{0,7},{1,8},{2,9},{3,10},{4,11},{5,12},{6,13},{7,14},{8,15},{9,16}... | collective-permute-start | bytes 196616
  505.8 1.6 concatenate.10
  (169 shorter events, 65.4 us)
Async XLA Ops:
  6.5 68.9 %all-gather.15.cloned.1.call-start = ((), (), s32[]{:S(2)}) async-start(), calls=%async_computation.4 | async-start | bytes 2162688 | tf_op jit(solution)/shard_map/all_gather | solution.py:84
  7.3 136.8 %all-gather.7.cloned.1.call-start = ((), (), s32[]{:S(2)}) async-start(), calls=%async_computation | async-start | bytes 3342336 | tf_op jit(solution)/shard_map/all_gather | solution.py:90
  8.0 208.8 %all-gather.9.cloned.1.call-start = ((), (), s32[]{:S(2)}) async-start(), calls=%async_computation.1 | async-start | bytes 1114112 | tf_op jit(solution)/shard_map/all_gather | solution.py:151
  8.7 283.0 %all-gather.11.cloned.1.call-start = ((), (), s32[]{:S(2)}) async-start(), calls=%async_computation.2 | async-start | bytes 4456448 | tf_op jit(solution)/shard_map/all_gather | solution.py:95
  9.3 375.0 %all-gather.13.cloned.1.call-start = ((), (), s32[]{:S(2)}) async-start(), calls=%async_computation.3 | async-start | bytes 4456448 | tf_op jit(solution)/shard_map/all_gather | solution.py:152
  9.9 0.5 copy-start.6
  77.6 66.4 %copy-start.7 = (f32[4096]{0:T(1024)S(1)}, f32[4096]{0:T(1024)}, u32[]{:S(2)}) copy-start(f32[4096]{0:T(1024)} %param.22) | copy-start | bytes 49156
  77.6 66.4 %copy-start.8 = (f32[4096]{0:T(1024)S(1)}, f32[4096]{0:T(1024)}, u32[]{:S(2)}) copy-start(f32[4096]{0:T(1024)} %param.21) | copy-start | bytes 49156
  77.6 66.4 %copy-start.11 = (f32[384]{0:T(512)S(1)}, f32[384]{0:T(512)}, u32[]{:S(2)}) copy-start(f32[384]{0:T(512)} %param.26) | copy-start | bytes 4612
  80.6 66.9 %copy-start.4 = (f32[192]{0:T(256)}, f32[192]{0:T(256)S(1)}, u32[]{:S(2)}) copy-start(f32[192]{0:T(256)S(1)} %add_rsqrt_fusion) | copy-start | bytes 2308
  147.5 1.4 copy-start.1
  216.7 167.6 %copy-start.5 = (f32[192]{0:T(256)S(1)}, f32[192]{0:T(256)}, u32[]{:S(2)}) copy-start(f32[192]{0:T(256)} %copy-done.4) | copy-start | bytes 2308
  216.7 167.6 %copy-start.9 = (f32[4096]{0:T(1024)S(1)}, f32[4096]{0:T(1024)}, u32[]{:S(2)}) copy-start(f32[4096]{0:T(1024)} %param.24) | copy-start | bytes 49156
  216.7 167.6 %copy-start.10 = (f32[4096]{0:T(1024)S(1)}, f32[4096]{0:T(1024)}, u32[]{:S(2)}) copy-start(f32[4096]{0:T(1024)} %param.23) | copy-start | bytes 49156
  216.7 167.6 %copy-start.12 = (f32[512]{0:T(512)S(1)}, f32[512]{0:T(512)}, u32[]{:S(2)}) copy-start(f32[512]{0:T(512)} %param.30) | copy-start | bytes 6148
  220.3 287.2 %copy-start = (bf16[6,4096]{1,0:T(8,128)(2,1)S(1)}, bf16[6,4096]{1,0:T(8,128)(2,1)}, u32[]{:S(2)}) copy-start(bf16[6,4096]{1,0:T(8,128)(2,1)} %param.20) | copy-start | bytes 147460
  220.3 287.2 %copy-start.2 = (f32[4096]{0:T(1024)S(1)}, f32[4096]{0:T(1024)}, u32[]{:S(2)}) copy-start(f32[4096]{0:T(1024)} %param.32) | copy-start | bytes 49156
  220.3 287.2 %copy-start.3 = (f32[4096]{0:T(1024)S(1)}, f32[4096]{0:T(1024)}, u32[]{:S(2)}) copy-start(f32[4096]{0:T(1024)} %param.28) | copy-start | bytes 49156
  477.1 15.2 %collective-permute-start = (bf16[8,4096]{1,0:T(8,128)(2,1)S(1)}, bf16[8,4096]{1,0:T(8,128)(2,1)S(1)}, u32[]{:S(2)}, u32[]{:S(2)}) collective-permute-start(bf16[8,4096]{1,0:T(8,128)(2,1)S(1)} %fusion.2), channel_id=1, source_target_pairs={{0,1},{1,2},{2,3},{3,4},{4,5},{5,6},{6,7},{7,8},{8,9},{9,10},{10,1... | collective-permute-start | bytes 196616
  480.6 16.8 %collective-permute-start.1 = (bf16[8,4096]{1,0:T(8,128)(2,1)S(1)}, bf16[8,4096]{1,0:T(8,128)(2,1)S(1)}, u32[]{:S(2)}, u32[]{:S(2)}) collective-permute-start(bf16[8,4096]{1,0:T(8,128)(2,1)S(1)} %fusion.2), channel_id=1, source_target_pairs={{0,2},{1,3},{2,4},{3,5},{4,6},{5,7},{6,8},{7,9},{8,10},{9,11},{10,... | collective-permute-start | bytes 196616
  481.9 4.9 collective-permute-start.7
  483.2 22.6 %collective-permute-start.2 = (bf16[8,4096]{1,0:T(8,128)(2,1)S(1)}, bf16[8,4096]{1,0:T(8,128)(2,1)S(1)}, u32[]{:S(2)}, u32[]{:S(2)}) collective-permute-start(bf16[8,4096]{1,0:T(8,128)(2,1)S(1)} %fusion.2), channel_id=1, source_target_pairs={{0,3},{1,4},{2,5},{3,6},{4,7},{5,8},{6,9},{7,10},{8,11},{9,12},{10... | collective-permute-start | bytes 196616
  484.5 21.3 %collective-permute-start.3 = (bf16[8,4096]{1,0:T(8,128)(2,1)S(1)}, bf16[8,4096]{1,0:T(8,128)(2,1)S(1)}, u32[]{:S(2)}, u32[]{:S(2)}) collective-permute-start(bf16[8,4096]{1,0:T(8,128)(2,1)S(1)} %fusion.2), channel_id=1, source_target_pairs={{0,4},{1,5},{2,6},{3,7},{4,8},{5,9},{6,10},{7,11},{8,12},{9,13},{1... | collective-permute-start | bytes 196616
  486.8 19.0 %collective-permute-start.4 = (bf16[8,4096]{1,0:T(8,128)(2,1)S(1)}, bf16[8,4096]{1,0:T(8,128)(2,1)S(1)}, u32[]{:S(2)}, u32[]{:S(2)}) collective-permute-start(bf16[8,4096]{1,0:T(8,128)(2,1)S(1)} %fusion.2), channel_id=1, source_target_pairs={{0,5},{1,6},{2,7},{3,8},{4,9},{5,10},{6,11},{7,12},{8,13},{9,14},{... | collective-permute-start | bytes 196616
  492.3 13.5 %collective-permute-start.5 = (bf16[8,4096]{1,0:T(8,128)(2,1)S(1)}, bf16[8,4096]{1,0:T(8,128)(2,1)S(1)}, u32[]{:S(2)}, u32[]{:S(2)}) collective-permute-start(bf16[8,4096]{1,0:T(8,128)(2,1)S(1)} %fusion.2), channel_id=1, source_target_pairs={{0,6},{1,7},{2,8},{3,9},{4,10},{5,11},{6,12},{7,13},{8,14},{9,15},... | collective-permute-start | bytes 196616
  497.4 8.4 %collective-permute-start.6 = (bf16[8,4096]{1,0:T(8,128)(2,1)S(1)}, bf16[8,4096]{1,0:T(8,128)(2,1)S(1)}, u32[]{:S(2)}, u32[]{:S(2)}) collective-permute-start(bf16[8,4096]{1,0:T(8,128)(2,1)S(1)} %fusion.2), channel_id=1, source_target_pairs={{0,7},{1,8},{2,9},{3,10},{4,11},{5,12},{6,13},{7,14},{8,15},{9,16}... | collective-permute-start | bytes 196616
Sparse Core Ops, SparseCore 0:
  10.5 64.8 all-gather.14
  77.5 66.4 all-gather.6
  146.0 66.7 all-gather.8
  214.7 76.9 all-gather.10
  293.6 90.6 all-gather.12
where the time goes:
time: 517 us; the launch traced here: 515 us
  waiting for transfers between devices  291 us (56%)
  blocking collectives  84.4 us (16%)
  matrix products  48.6 us (9%)
  starting transfers between devices  26.8 us (5%)
  local copies, waits for them, and re-layouts  26.2 us (5%)
  other arithmetic  23.1 us (4%)
  between operations  14.2 us (3%)
    all_gather x1, waiting for transfers between devices, body(): lax.all_gather(w_down, 'tok', axis=1, tiled=True)  92.5 us
    unnamed x1, blocking collectives  84.4 us
    all_gather x1, waiting for transfers between devices, body(): lax.all_gather(w_up, 'tok', axis=0, tiled=True)  71.5 us
    all_gather x1, waiting for transfers between devices, body(): lax.all_gather(w_qkv, 'tok', axis=0, tiled=True)  63.4 us
    all_gather x1, waiting for transfers between devices, body(): whole = lax.all_gather(tokens, 'head', axis=0, tiled=True)  60.5 us
    unnamed x8, starting transfers between devices  26.7 us
    dot_general x12, matrix products, first_pass(): raw = jnp.dot(queries, keys.T, preferred_element_type=jnp.float32) * scale  15.7 us
    dot_general x12, matrix products, second_pass(): jnp.dot(weights.astype(jnp.bfloat16), values, preferred_element_type=jnp....  15.6 us
  transfers between devices with their start and end apart: 13, of which 4 were waited for; matrix products, arithmetic and copies ran while one was open for 17% of the time, Pallas kernels for 0%

commit v1 on v0

--- a/solution.py
+++ b/solution.py
@@ -81,21 +81,23 @@
     cache_lengths,
 ):
     scale = HD ** (-0.5)
+    width_qkv = w_qkv.shape[1]
+    width_up = w_up.shape[1]
+    width_dense = w_dense.shape[0]
+    packed = jnp.concatenate([w_qkv, w_up, w_dense.T, w_down.T], axis=1)
+    gathered = lax.all_gather(packed, "tok", axis=0, tiled=False)
+    parts = gathered.shape[0] * gathered.shape[1]
+    qkv_full = gathered[:, :, :width_qkv].reshape(parts, width_qkv)
+    up_full = gathered[:, :, width_qkv : width_qkv + width_up].reshape(parts, width_up)
+    offset = width_qkv + width_up
+    dense_t = gathered[:, :, offset : offset + width_dense].reshape(parts, width_dense)
+    down_t = gathered[:, :, offset + width_dense :].reshape(parts, -1)
     whole = lax.all_gather(tokens, "head", axis=0, tiled=True)
     normed_one = layer_norm(whole, ln1_gain, ln1_bias).astype(jnp.bfloat16)
     normed_two = layer_norm(whole, ln2_gain, ln2_bias).astype(jnp.bfloat16)
     rows_total = whole.shape[0]
-    projected = jnp.dot(
-        normed_one,
-        lax.all_gather(w_qkv, "tok", axis=0, tiled=True),
-        preferred_element_type=jnp.float32,
-    )
-    upward = jnp.dot(
-        normed_two,
-        lax.all_gather(w_up, "tok", axis=0, tiled=True),
-        preferred_element_type=jnp.float32,
-    )
-    projected = projected + b_qkv
+    projected = jnp.dot(normed_one, qkv_full, preferred_element_type=jnp.float32) + b_qkv
+    upward = jnp.dot(normed_two, up_full, preferred_element_type=jnp.float32)
     lengths_row = cache_lengths[0]
     query_owner, query_place = token_layout(lengths_row, rows_total)
     queries = rotate(projected[:, :HD], query_place).astype(jnp.bfloat16)
@@ -104,62 +106,30 @@
     hidden = jax.nn.gelu(upward + b_up, approximate=False).astype(jnp.bfloat16)
     slots = k_cache.shape[0]
     slot_owner, slot_place = slot_layout(lengths_row, slots)
-    block = 512
-    while slots % block:
-        block = block // 2
-    number = slots // block
-    indices = jnp.arange(number, dtype=jnp.int32)
-    key_blocks = k_cache.reshape(number, block, HD)
-    value_blocks = v_cache.reshape(number, block, HD)
-    owner_blocks = slot_owner.reshape(number, block)
-    place_blocks = slot_place.reshape(number, block)
+    cache_scores = jnp.dot(queries, k_cache.T, preferred_element_type=jnp.float32) * scale
+    cache_scores = jnp.where(
+        visible(query_owner, query_place, slot_owner, slot_place), cache_scores, -jnp.inf
+    )
     new_scores = jnp.dot(queries, new_keys.T, preferred_element_type=jnp.float32) * scale
     new_scores = jnp.where(
         visible(query_owner, query_place, query_owner, query_place), new_scores, -jnp.inf
     )
-
-    def first_pass(top, items):
-        index, keys, block_owner, block_place = items
-        raw = jnp.dot(queries, keys.T, preferred_element_type=jnp.float32) * scale
-        scores = jnp.where(
-            visible(query_owner, query_place, block_owner, block_place), raw, -jnp.inf
-        )
-        return (jnp.maximum(top, jnp.max(scores, axis=1)), scores)
-
-    top, stored = lax.scan(
-        first_pass, jnp.max(new_scores, axis=1), (indices, key_blocks, owner_blocks, place_blocks)
-    )
+    top = jnp.maximum(jnp.max(cache_scores, axis=1), jnp.max(new_scores, axis=1))
+    cache_weights = jnp.exp(cache_scores - top[:, None])
     new_weights = jnp.exp(new_scores - top[:, None])
-    start_state = (
-        jnp.sum(new_weights, axis=1),
-        jnp.dot(new_weights.astype(jnp.bfloat16), new_values, preferred_element_type=jnp.float32),
-    )
-
-    def second_pass(state, items):
-        index, scores, values = items
-        weights = jnp.exp(scores - top[:, None])
-        state = (
-            state[0] + jnp.sum(weights, axis=1),
-            state[1]
-            + jnp.dot(weights.astype(jnp.bfloat16), values, preferred_element_type=jnp.float32),
-        )
-        return (state, None)
-
-    final, unused = lax.scan(second_pass, start_state, (indices, stored, value_blocks))
-    attention = (final[1] / final[0][:, None]).astype(jnp.bfloat16)
-    dense_full, down_full = (
-        lax.all_gather(w_dense, "tok", axis=1, tiled=True),
-        lax.all_gather(w_down, "tok", axis=1, tiled=True),
-    )
-    partial_value = lax.psum_scatter(
-        (
-            jnp.dot(attention, dense_full, preferred_element_type=jnp.float32)
-            + jnp.dot(hidden, down_full, preferred_element_type=jnp.float32)
-        ).astype(jnp.bfloat16),
-        "head",
-        scatter_dimension=0,
-        tiled=True,
-    ).astype(jnp.float32)
+    total = jnp.sum(cache_weights, axis=1) + jnp.sum(new_weights, axis=1)
+    summed = jnp.dot(
+        cache_weights.astype(jnp.bfloat16), v_cache, preferred_element_type=jnp.float32
+    ) + jnp.dot(new_weights.astype(jnp.bfloat16), new_values, preferred_element_type=jnp.float32)
+    attention = (summed / total[:, None]).astype(jnp.bfloat16)
+    contract = (((1,), (1,)), ((), ()))
+    partial = lax.dot_general(
+        attention, dense_t, contract, preferred_element_type=jnp.float32
+    ) + lax.dot_general(hidden, down_t, contract, preferred_element_type=jnp.float32)
+    heads = lax.axis_size("head")
+    partial = partial.astype(jnp.bfloat16).reshape(heads, rows_total // heads, -1)
+    partial_value = lax.psum_scatter(partial, "head", scatter_dimension=0, tiled=True)
+    partial_value = partial_value.reshape(tokens.shape).astype(jnp.float32)
     mixed = tokens.astype(jnp.float32) + partial_value + b_dense + b_down
     return mixed.astype(jnp.bfloat16)
 

time: 517 us -> 393 us (0.76)
  blocking collectives: 84.4 us -> 0 us
  waiting for transfers between devices: 291 us -> 323 us
  matrix products: 48.6 us -> 18.4 us
  starting transfers between devices: 26.8 us -> 0.08 us
  other arithmetic: 23.1 us -> 9.59 us
    reduce_scatter x0 -> x1, waiting for transfers between devices: none -> 104 us  [body(): lax.psum_scatter(partial, 'head', scatter_dimension=0, tiled=True)]
    unnamed x1 -> x0, blocking collectives: 84.4 us -> none
    all_gather x4 -> x1, waiting for transfers between devices: 227 us -> 155 us  [body(): gathered = lax.all_gather(packed, 'tok', axis=0, tiled=False)]
    dot_general x27 -> x4, matrix products: 46.5 us -> 18 us  [the longest x1 8.67 us: body(): lax.dot_general(hidden, down_t, contract, preferred_element_type=jnp.floa...]
    unnamed x8 -> x0, starting transfers between devices: 26.7 us -> none
    unnamed x30 -> x37, local copies, waits for them, and re-layouts: 4.13 us -> 21.5 us
    reduce_sum x13 -> x3, other arithmetic: 14.6 us -> 1.24 us  [the longest x2 0.86 us: body(): total = jnp.sum(cache_weights, axis=1) + jnp.sum(new_weights, axis=1)]
    dynamic_update_slice x12 -> x0, local copies, waits for them, and re-layouts: 9.43 us -> none  [body(): lax.scan(first_pass, jnp.max(new_scores, axis=1), (indices, key_blocks, o...]
  transfers between devices with their start and end apart: 13 -> 3, of which waited for: 4 -> 3; matrix products, arithmetic and copies ran while one was open for 17% -> 3% of each run, Pallas kernels for 0% -> 0%
where the time goes in v1:
time: 393 us
  waiting for transfers between devices  323 us (82%)
  local copies, waits for them, and re-layouts  28.1 us (7%)
  matrix products  18.4 us (5%)
  between operations  13.4 us (3%)
  other arithmetic  9.59 us (2%)
    all_gather x1, waiting for transfers between devices, body(): gathered = lax.all_gather(packed, 'tok', axis=0, tiled=False)  155 us
    reduce_scatter x1, waiting for transfers between devices, body(): lax.psum_scatter(partial, 'head', scatter_dimension=0, tiled=True)  104 us
    all_gather x1, waiting for transfers between devices, body(): whole = lax.all_gather(tokens, 'head', axis=0, tiled=True)  63.2 us
    unnamed x37, local copies, waits for them, and re-layouts  21.5 us
    dot_general x1, matrix products, body(): lax.dot_general(hidden, down_t, contract, preferred_element_type=jnp.floa...  8.67 us
  transfers between devices with their start and end apart: 3, of which 3 were waited for; matrix products, arithmetic and copies ran while one was open for 3% of the time, Pallas kernels for 0%

profile of v1, /device:TPU:1, one launch (start us, length us, event | category | flops | bytes accessed | tf_op | source)
XLA Modules:
  0.0 392.5 jit_solution(7284414699249301596)
XLA Ops:
  6.5 0.7 all-gather.7.cloned.1.call-update
  7.3 1.1 copy.26
  8.4 1.1 copy.25
  9.5 1.9 pad_maximum_fusion
  11.4 0.2 reduce-window_clone.1
  11.8 0.4 convert_reduce_fusion.1
  12.2 63.2 %all-gather.7.cloned.1.call-done = bf16[32,6,4096]{2,1,0:T(8,128)(2,1)} async-done(((bf16[1,6,4096]{2,1,0:T(8,128)(2,1)}), bf16[32,6,4096]{2,1,0:T(8,128)(2,1)}) %all-gather.7.cloned.1.call-update) | async-done | bytes 1572880 | tf_op jit(solution)/shard_map/all_gather | solution.py:95
  75.5 2.1 convert_reduce_fusion
  77.5 0.1 reshape.130
  77.7 3.8 reshape.127
  81.4 2.3 multiply_reduce_fusion
  83.8 154.9 %all-gather.5.cloned.1.call-done = bf16[4096,1536]{0,1:T(8,128)(2,1)} async-done(((bf16[256,1536]{0,1:T(8,128)(2,1)}), bf16[4096,1536]{0,1:T(8,128)(2,1)}) %all-gather.5.cloned.1.call-update) | async-done | bytes 12582928 | tf_op jit(solution)/shard_map/all_gather | solution.py:88
  238.6 7.9 %copy.29 = bf16[192,8,16,256]{3,2,1,0:T(8,128)(2,1)S(1)} copy(bf16[192,8,16,256]{3,1,2,0:T(8,128)(2,1)} %bitcast.40) | data formatting | bytes 25165824
  246.6 0.2 slice.55
  246.9 1.6 copy.30
  248.5 0.3 copy-done.3
  248.8 1.2 fusion.144
  250.0 0.1 fusion.101
  250.1 0.3 fusion.146
  250.4 2.7 fusion.145
  253.1 0.2 fusion.82
  253.4 0.8 fusion.142
  254.2 0.4 copy.31
  254.6 0.6 copy-done.2
  255.2 0.8 fusion.4
  256.0 4.3 %copy.33 = bf16[64,8,16,256]{3,1,2,0:T(8,128)(2,1)} copy(bf16[64,8,16,256]{3,2,1,0:T(8,128)(2,1)S(1)} %bitcast.39) | data formatting | bytes 8388608
  260.3 4.3 %copy.32 = bf16[64,8,16,256]{3,1,2,0:T(8,128)(2,1)} copy(bf16[64,8,16,256]{3,2,1,0:T(8,128)(2,1)S(1)} %bitcast.38) | data formatting | bytes 8388608
  264.6 5.4 %fusion.32 = f32[192,4096]{1,0:T(8,128)} fusion(bf16[4096,128]{0,1:T(8,128)(2,1)S(1)} %bitcast.42, f32[192,128]{1,0:T(8,128)S(1)} %fusion.82, bf16[6144,128]{1,0:T(8,128)(2,1)S(1)} %copy-done.4, f32[192,6144]{1,0:T(8,128)} %copy-done.2, f32[192]{0:T(256)S(1)} %max.37, f32[192]{0:T(256)S(1)} %add.133), kind=kOutput, calls=%fused_computation.32 | convolution fusion | flops 505749504 | bytes 10585600 | tf_op jit(solution)/shard_map/dot_general | solution.py:126
  270.0 8.7 %fusion.1 = bf16[192,4096]{1,0:T(8,128)(2,1)S(1)} fusion(f32[192,4096]{1,0:T(8,128)} %fusion.32, bf16[4096,512]{0,1:T(8,128)(2,1)} %bitcast.43, bf16[4096,512]{0,1:T(8,128)(2,1)} %bitcast.44, f32[192,4096]{1,0:T(8,128)} %reshape.127, f32[4096]{0:T(1024)S(1)} %copy-done.11, f32[4096]{0:T(1024)S(1)} %copy-done.12, f32[192]{0:T(256)S(1)} %add_rsqrt_fusion, ...), kind=kOutput, calls=%fused_computation.3 | convolution fusion | flops 1622605824 | bytes 16289280 | tf_op jit(solution)/shard_map/dot_general | solution.py:128
  278.8 1.6 reshape.122
  280.4 104.1 %reduce-scatter.2.cloned.1.call-done = bf16[1,6,4096]{2,1,0:T(8,128)(2,1)} async-done(((bf16[32,6,4096]{2,1,0:T(8,128)(2,1)}), bf16[1,6,4096]{2,1,0:T(8,128)(2,1)}) %reduce-scatter.2.cloned.1.call-update) | async-done | bytes 49168 | tf_op jit(solution)/shard_map/reduce_scatter | solution.py:131
  384.5 1.5 fusion.81
  (48 shorter events, 0.5 us)
Async XLA Ops:
  6.5 243.9 %copy-start = (bf16[6144,128]{1,0:T(8,128)(2,1)S(1)}, bf16[6144,128]{1,0:T(8,128)(2,1)}, u32[]{:S(2)}) copy-start(bf16[6144,128]{1,0:T(8,128)(2,1)} %param.29) | copy-start | bytes 4718596
  6.5 4.9 %copy-start.8 = (s32[1,33]{1,0:T(1,128)S(1)}, s32[1,33]{1,0:T(1,128)}, u32[]{:S(2)}) copy-start(s32[1,33]{1,0:T(1,128)} %param.31) | copy-start | bytes 400
  6.5 68.9 %all-gather.7.cloned.1.call-start = ((), (), s32[]{:S(2)}) async-start(), calls=%async_computation.3 | async-start | bytes 2162688 | tf_op jit(solution)/shard_map/all_gather | solution.py:95
  7.3 231.4 %all-gather.5.cloned.1.call-start = ((), (), s32[]{:S(2)}) async-start(), calls=%async_computation.2 | async-start | bytes 13369344 | tf_op jit(solution)/shard_map/all_gather | solution.py:88
  11.4 373.1 %reduce-scatter.2.cloned.1.call-start = ((), (), s32[]{:S(2)}) async-start(), calls=%async_computation.1 | async-start | bytes 2162688 | tf_op jit(solution)/shard_map/reduce_scatter | solution.py:131
  246.9 1.9 copy-start.3
  246.9 1.9 copy-start.9
  246.9 1.9 copy-start.10
  246.9 1.9 copy-start.13
  253.1 2.2 copy-start.2
  260.3 4.3 %copy-start.4 = (bf16[6144,128]{1,0:T(8,128)(2,1)S(1)}, bf16[6144,128]{1,0:T(8,128)(2,1)}, u32[]{:S(2)}) copy-start(bf16[6144,128]{1,0:T(8,128)(2,1)} %param.30) | copy-start | bytes 4718596
  264.6 5.4 %copy-start.11 = (f32[4096]{0:T(1024)S(1)}, f32[4096]{0:T(1024)}, u32[]{:S(2)}) copy-start(f32[4096]{0:T(1024)} %param.20) | copy-start | bytes 49156
  264.6 5.4 %copy-start.12 = (f32[4096]{0:T(1024)S(1)}, f32[4096]{0:T(1024)}, u32[]{:S(2)}) copy-start(f32[4096]{0:T(1024)} %param.19) | copy-start | bytes 49156
  264.6 5.4 %copy-start.14 = (f32[512]{0:T(512)S(1)}, f32[512]{0:T(512)}, u32[]{:S(2)}) copy-start(f32[512]{0:T(512)} %param.26) | copy-start | bytes 6148
  270.0 116.0 %copy-start.1 = (bf16[6144,128]{1,0:T(8,128)(2,1)S(1)}, bf16[6144,128]{1,0:T(8,128)(2,1)}, u32[]{:S(2)}) copy-start(bf16[6144,128]{1,0:T(8,128)(2,1)} %param.29) | copy-start | bytes 4718596
  278.7 105.8 %copy-start.5 = (bf16[6,4096]{1,0:T(8,128)(2,1)S(1)}, bf16[6,4096]{1,0:T(8,128)(2,1)}, u32[]{:S(2)}) copy-start(bf16[6,4096]{1,0:T(8,128)(2,1)} %param.16) | copy-start | bytes 147460
  278.7 105.8 %copy-start.6 = (f32[4096]{0:T(1024)S(1)}, f32[4096]{0:T(1024)}, u32[]{:S(2)}) copy-start(f32[4096]{0:T(1024)} %param.28) | copy-start | bytes 49156
  278.7 105.8 %copy-start.7 = (f32[4096]{0:T(1024)S(1)}, f32[4096]{0:T(1024)}, u32[]{:S(2)}) copy-start(f32[4096]{0:T(1024)} %param.24) | copy-start | bytes 49156
Sparse Core Ops, SparseCore 0:
  10.5 64.9 all-gather.6
  77.5 161.1 all-gather.4
  280.5 103.9 reduce-scatter.1
